TPU v7x, 256 devices: a whole 4x4x8 slice. The times are simulated.
256 devices in a mesh: dp: 32 (over y, z), mp: 8 (over x, core).
Axes of the slice: x: 4, y: 4, z: 8, core: 2. Of those that a mesh axis runs over, the one named last changes fastest.
Arguments:
- hidden: bfloat16 [512, 32, 1024], P(('dp', 'mp')), may hold values from -96 to 96, as said below
- query_weight: bfloat16 [1024, 1024], P('dp', 'mp'), may hold values from -0.1875 to 0.1875
- w_key: bfloat16 [1024, 1024], P('dp', 'mp'), may hold values from -0.1875 to 0.1875
- w_value: bfloat16 [1024, 1024], P('dp', 'mp'), may hold values from -0.1875 to 0.1875
- rel_table: bfloat16 [512, 1024], P('dp'), may hold values from -6 to 6
- rel_bucket: int32 [32, 32], replicated, may hold values from 0 to 511
- w_out: bfloat16 [1024, 1024], P('mp', 'dp'), may hold values from -0.1875 to 0.1875
- w_up: bfloat16 [1024, 4096], P('dp', 'mp'), may hold values from -0.1875 to 0.1875
- w_down: bfloat16 [4096, 1024], P('mp', 'dp'), may hold values from -0.09375 to 0.09375
- w_proj: bfloat16 [1024, 128], P(('dp', 'mp')), may hold values from -0.1875 to 0.1875
- pages: bfloat16 [8192, 128, 128], P('dp'), may hold values from -0.59765625 to 0.59765625
- page_len: int32 [8192], P('dp'), may hold values from 1 to 128
- slot_per_page: int32 [8192], replicated, may hold values from 0 to 8191, as said below
- candidates: int32 [512, 16, 4], P(('dp', 'mp')), may hold values from 0 to 8191, as said below
Outputs:
- query_vectors: bfloat16 [512, 32, 128], P(('dp', 'mp'))
- scores: float32 [512, 16], P(('dp', 'mp'))
Inputs may be any that keep to these rules, and one draw needn't show every extreme that they name: slot_per_page is a permutation of the slots; the page in slot s is held by index s // 256 of dp. `candidates`: among the 128 page ids of the 2 queries of one device (queries in aligned blocks of 2), at most 8 have slots held by any one index of dp, and in every such block some index of dp holds exactly 8 of them. `hidden`: token states are finite.
All inputs are finite; a program needn't handle non-finite values.
Results may differ from a plain program's by a relative error of at most 0.025.
Values may be sent and summed in bfloat16 or wider, within the bound.
No kernel may reach another device: no remote copies, remote signals or barrier semaphores. Data moves between devices by JAX's collectives and lax.ppermute only.
A program may use at most 64 MiB of HBM per device.

v0:
```python
import jax
import jax.numpy as jnp
from jax import lax
from jax.sharding import PartitionSpec as P

HD = 64


def layer_norm(value):
    mean = jnp.mean(value, axis=-1, keepdims=True)
    centered = value - mean
    var = jnp.mean(centered * centered, axis=-1, keepdims=True)
    return centered / jnp.sqrt(var + 1e-07)


def add_rows(left, piece):
    return jnp.dot(left, piece, preferred_element_type=jnp.float32)


def return_maxima(maxima):
    return lax.all_to_all(
        maxima.astype(jnp.bfloat16), "dp", split_axis=0, concat_axis=0, tiled=True
    ).astype(maxima.dtype)


def body(
    hidden,
    query_weight,
    w_key,
    w_value,
    rel_table,
    rel_bucket,
    w_out,
    w_up,
    w_down,
    w_proj,
    pages,
    page_len,
    slot_per_page,
    candidates,
):
    qry_dev, qlen, width = hidden.shape
    heads_local = query_weight.shape[1] // HD
    cols = query_weight.shape[1]
    tokens = lax.all_gather(hidden, "mp", axis=0, tiled=True)
    group = tokens.shape[0]
    flat = tokens.reshape(group * qlen, width)
    left_rel = lax.all_gather(rel_table, "dp", axis=0, tiled=True)
    pieces = (
        lax.all_gather(query_weight, "dp", axis=0, tiled=True),
        lax.all_gather(w_key, "dp", axis=0, tiled=True),
        lax.all_gather(w_value, "dp", axis=0, tiled=True),
    )
    qsum = add_rows(flat, pieces[0])
    ksum = add_rows(flat, pieces[1])
    vsum = add_rows(flat, pieces[2])
    qrsum = add_rows(left_rel, pieces[0])
    krsum = add_rows(left_rel, pieces[1])
    rel_q = qrsum.astype(jnp.bfloat16)
    rel_k = krsum.astype(jnp.bfloat16)
    nbuck = rel_q.shape[0]
    qx = qsum.astype(jnp.bfloat16).reshape(group, qlen, heads_local, HD)
    kx = ksum.astype(jnp.bfloat16).reshape(group, qlen, heads_local, HD)
    vx = vsum.astype(jnp.bfloat16).reshape(group, qlen, heads_local, HD)
    rel_q = rel_q.reshape(nbuck, heads_local, HD)
    rel_k = rel_k.reshape(nbuck, heads_local, HD)
    onehot = (rel_bucket[:, :, None] == jnp.arange(nbuck, dtype=jnp.int32)[None, None, :]).astype(
        jnp.float32
    )
    scale = 1.0 / jnp.sqrt(jnp.float32(3 * HD))
    content = jnp.einsum("qihd,qjhd->qhij", qx, kx, preferred_element_type=jnp.float32)
    along_axis_name = jnp.einsum("qihd,bhd->qhib", qx, rel_k, preferred_element_type=jnp.float32)
    c2p = jnp.einsum("qhib,ijb->qhij", along_axis_name, onehot, precision=lax.Precision.HIGHEST)
    back = jnp.einsum("qjhd,bhd->qhjb", kx, rel_q, preferred_element_type=jnp.float32)
    p2c = jnp.einsum("qhjb,jib->qhij", back, onehot, precision=lax.Precision.HIGHEST)
    logits = (content + c2p + p2c) * scale
    probs = jax.nn.softmax(logits, axis=-1).astype(jnp.bfloat16)
    context_rows = jnp.einsum("qhij,qjhd->qihd", probs, vx, preferred_element_type=jnp.float32)
    context_rows = context_rows.astype(jnp.bfloat16).reshape(group * qlen, cols)
    attn_terms = jnp.dot(
        context_rows,
        lax.all_gather(w_out, "dp", axis=1, tiled=True),
        preferred_element_type=jnp.float32,
    )
    attn = lax.psum_scatter(
        attn_terms.astype(jnp.bfloat16), "mp", scatter_dimension=0, tiled=True
    ).astype(jnp.float32)
    own = hidden.reshape(qry_dev * qlen, width).astype(jnp.float32)
    mid = layer_norm(own + attn).astype(jnp.bfloat16)
    mid_all = lax.all_gather(mid, "mp", axis=0, tiled=True)
    up = add_rows(mid_all, lax.all_gather(w_up, "dp", axis=0, tiled=True))
    inner = jax.nn.gelu(up, approximate=False).astype(jnp.bfloat16)
    down_terms = jnp.dot(
        inner, lax.all_gather(w_down, "dp", axis=1, tiled=True), preferred_element_type=jnp.float32
    )
    mlp = lax.psum_scatter(
        down_terms.astype(jnp.bfloat16), "mp", scatter_dimension=0, tiled=True
    ).astype(jnp.float32)
    state = layer_norm(mid.astype(jnp.float32) + mlp).astype(jnp.bfloat16)
    width_out = w_proj.shape[1]
    proj = add_rows(state, lax.all_gather(w_proj, ("dp", "mp"), axis=0, tiled=True))
    vectors = (proj / jnp.sqrt(jnp.sum(proj * proj, axis=-1, keepdims=True) + 1e-06)).astype(
        jnp.bfloat16
    )
    vectors = vectors.reshape(qry_dev, qlen, width_out)
    page_owners = lax.axis_size("dp")
    pg_dev = pages.shape[0]
    ptok = pages.shape[1]
    ncand, ppc = (candidates.shape[1], candidates.shape[2])
    req = qry_dev * ncand * ppc
    cap = 2 * req // page_owners
    slots = slot_per_page[candidates.reshape(req)]
    dest = slots // pg_dev
    local = slots % pg_dev
    query_of = jnp.arange(req, dtype=jnp.int32) // (ncand * ppc)
    member = (dest[:, None] == jnp.arange(page_owners, dtype=jnp.int32)[None, :]).astype(jnp.int32)
    place = jnp.sum((jnp.cumsum(member, axis=0) - 1) * member, axis=1)
    index = dest * cap + place
    codes = jnp.full((page_owners * cap,), -1, jnp.int32).at[index].set(query_of * pg_dev + local)
    codes = codes.reshape(page_owners, cap)
    token_positions = jnp.arange(ptok, dtype=jnp.int32)
    rows_out = (
        jnp.zeros((page_owners * cap, qlen, width_out), jnp.bfloat16)
        .at[index]
        .set(vectors[query_of])
    )
    rows_out = rows_out.reshape(page_owners, cap, qlen, width_out)
    where_local = lax.all_to_all(codes, "dp", split_axis=0, concat_axis=0, tiled=True) % pg_dev
    chosen = pages[where_local]
    lens = page_len[where_local]
    sim = jnp.einsum(
        "snie,snte->snit",
        lax.all_to_all(rows_out, "dp", split_axis=0, concat_axis=0, tiled=True),
        chosen,
        preferred_element_type=jnp.float32,
    )
    valid = token_positions[None, None, None, :] < lens[:, :, None, None]
    returned = return_maxima(jnp.max(jnp.where(valid, sim, -1e30), axis=-1))
    best = returned.reshape(page_owners * cap, qlen)[index]
    best = best.reshape(qry_dev, ncand, ppc, qlen)
    scores = jnp.sum(jnp.max(best, axis=2), axis=-1)
    return (vectors, scores)


def solution(mesh):
    in_specs = (
        P(("dp", "mp"), None, None),
        P("dp", "mp"),
        P("dp", "mp"),
        P("dp", "mp"),
        P("dp", None),
        P(),
        P("mp", "dp"),
        P("dp", "mp"),
        P("mp", "dp"),
        P(("dp", "mp"), None),
        P("dp", None, None),
        P("dp"),
        P(),
        P(("dp", "mp"), None, None),
    )
    out_specs = (P(("dp", "mp"), None, None), P(("dp", "mp"), None))
    return jax.shard_map(body, mesh=mesh, in_specs=in_specs, out_specs=out_specs, check_vma=False)
```

profile of v0, /device:TPU:1, one launch (start us, length us, event | category | flops | bytes accessed | tf_op | source)
XLA Modules:
  0.0 620.8 jit_solution(7747046523202727993)
XLA Ops:
  8.7 41.4 %all_gather.32 = bf16[1024,128]{1,0:T(8,128)(2,1)S(1)} all-gather(bf16[32,128]{1,0:T(8,128)(2,1)} %param.15), channel_id=1, replica_groups=mesh['dp'=32,'mp'=8] {'dp'}, dimensions={0}, use_global_device_ids=true | all-gather | bytes 270336 | tf_op jit(solution)/shard_map/all_gather | solution.py:50
  50.1 38.1 %all_gather.33 = bf16[1024,128]{1,0:T(8,128)(2,1)S(1)} all-gather(bf16[32,128]{1,0:T(8,128)(2,1)} %param.16), channel_id=1, replica_groups=mesh['dp'=32,'mp'=8] {'dp'}, dimensions={0}, use_global_device_ids=true | all-gather | bytes 270336 | tf_op jit(solution)/shard_map/all_gather | solution.py:51
  88.1 37.2 %all_gather.31 = bf16[1024,128]{1,0:T(8,128)(2,1)S(1)} all-gather(bf16[32,128]{1,0:T(8,128)(2,1)} %param.17), channel_id=1, replica_groups=mesh['dp'=32,'mp'=8] {'dp'}, dimensions={0}, use_global_device_ids=true | all-gather | bytes 270336 | tf_op jit(solution)/shard_map/all_gather | solution.py:52
  125.3 35.7 %all_gather.35 = bf16[128,1024]{0,1:T(8,128)(2,1)S(1)} all-gather(bf16[128,32]{0,1:T(8,128)(2,1)} %param.20), channel_id=1, replica_groups=mesh['dp'=32,'mp'=8] {'dp'}, dimensions={1}, use_global_device_ids=true | all-gather | bytes 270336 | tf_op jit(solution)/shard_map/all_gather | solution.py:82
  161.0 1.7 convolution_convert_fusion.6
  162.9 1.7 convolution_convert_fusion.5
  165.3 1.7 convolution_convert_fusion.4
  167.6 1.4 fusion.3
  170.2 1.4 fusion.1
  173.0 1.4 convolution_convert_fusion
  175.7 73.5 %reduce-scatter.3.cloned.1.call-done = bf16[64,1024]{1,0:T(8,128)(2,1)} async-done(((bf16[512,1024]{1,0:T(8,128)(2,1)}), bf16[64,1024]{1,0:T(8,128)(2,1)}) %reduce-scatter.3.cloned.1.call-update) | async-done | bytes 131088 | tf_op jit(solution)/shard_map/reduce_scatter | solution.py:85
  249.2 1.0 fusion.67
  250.3 1.1 multiply_reduce_fusion.1
  251.4 1.7 divide_convert_fusion.3
  253.4 70.8 %all-gather.13.cloned.1.call-done = bf16[1024,512]{1,0:T(8,128)(2,1)} async-done(((bf16[32,512]{1,0:T(8,128)(2,1)}), bf16[1024,512]{1,0:T(8,128)(2,1)}) %all-gather.13.cloned.1.call-update) | async-done | bytes 1048592 | tf_op jit(solution)/shard_map/all_gather | solution.py:91
  324.1 76.3 %all-gather.15.cloned.1.call-done = bf16[512,1024]{0,1:T(8,128)(2,1)} async-done(((bf16[512,32]{0,1:T(8,128)(2,1)}), bf16[512,1024]{0,1:T(8,128)(2,1)}) %all-gather.15.cloned.1.call-update) | async-done | bytes 1048592 | tf_op jit(solution)/shard_map/all_gather | solution.py:94
  400.4 30.5 %all-gather.11.cloned.1.call-done = bf16[512,1024]{1,0:T(8,128)(2,1)} async-done(((bf16[64,1024]{1,0:T(8,128)(2,1)}), bf16[512,1024]{1,0:T(8,128)(2,1)}) %all-gather.11.cloned.1.call-update) | async-done | bytes 1048592 | tf_op jit(solution)/shard_map/all_gather | solution.py:90
  430.9 6.2 %convolution_convert_fusion.1 = bf16[512,1024]{1,0:T(8,128)(2,1)} fusion(bf16[512,1024]{0,1:T(8,128)(2,1)} %all-gather.15.cloned.1.call-done, bf16[512,1024]{1,0:T(8,128)(2,1)} %all-gather.11.cloned.1.call-done, bf16[1024,512]{1,0:T(8,128)(2,1)} %all-gather.13.cloned.1.call-done), kind=kOutput, calls=%fused_computation.17 | convolution fusion | flops 1091305472 | bytes 4194304 | tf_op jit(solution)/shard_map/dot_general | solution.py:93
  437.4 1.1 gather_fusion
  440.7 9.6 %all-to-all-start = ((s32[32,1,8]{2,1,0:T(1,128)}), s32[32,1,8]{2,1,0:T(1,128)S(1)}, u32[]{:S(2)}, u32[]{:S(2)}) async-start(s32[32,1,8]{2,1,0:T(1,128)} %bitcast.21), calls=%async_computation.2 | async-start | bytes 32768 | tf_op jit(solution)/shard_map/all_to_all | solution.py:128
  450.3 62.5 %all-gather = bf16[256,4,128]{2,1,0:T(4,128)(2,1)S(1)} all-gather(bf16[1,4,128]{2,1,0:T(4,128)(2,1)S(1)} %bitcast.96), channel_id=1, replica_groups=mesh['dp'=32,'mp'=8] {'dp','mp'}, dimensions={0}, use_global_device_ids=true | all-gather | bytes 263168 | tf_op jit(solution)/shard_map/all_gather | solution.py:101
  513.9 1.1 multiply_reduce_fusion
  515.0 1.3 multiply_reduce_fusion.2
  517.2 1.7 broadcast_in_dim.14
  518.8 13.7 %scatter_fusion = bf16[256,32,128]{2,1,0:T(8,128)(2,1)} fusion(bf16[256,32,128]{2,1,0:T(8,128)(2,1)} %broadcast_in_dim.14, s32[128]{0:T(128)S(1)} %fusion.75, bf16[128,32,128]{2,1,0:T(8,128)(2,1)S(1)} %gather_fusion.2), kind=kCustom, calls=%fused_computation.6 | custom fusion | bytes 3146240 | tf_op jit(solution)/shard_map/scatter | solution.py:125
  532.5 6.3 %all-to-all-start.1 = ((bf16[32,8,32,128]{3,2,1,0:T(8,128)(2,1)}), bf16[32,8,32,128]{3,2,1,0:T(8,128)(2,1)S(1)}, u32[]{:S(2)}, u32[]{:S(2)}) async-start(bf16[32,8,32,128]{3,2,1,0:T(8,128)(2,1)} %bitcast.24), calls=%async_computation.3 | async-start | bytes 4194304 | tf_op jit(solution)/shard_map/all_to_all | solution.py:133
  538.9 11.8 %gather_fusion.3 = bf16[256,128,128]{2,1,0:T(8,128)(2,1)} fusion(bf16[256,128,128]{2,1,0:T(8,128)(2,1)} %param.24, s32[1024]{0:T(1024)S(1)} %pad_clamp_fusion.2), kind=kCustom, calls=%fused_computation.3 | custom fusion | bytes 16778240 | tf_op jit(solution)/shard_map/gather | solution.py:129
  550.8 1.9 gather_fusion.1
  552.9 34.5 %all-to-all-done.1 = bf16[32,8,32,128]{3,2,1,0:T(8,128)(2,1)S(1)} async-done(((bf16[32,8,32,128]{3,2,1,0:T(8,128)(2,1)}), bf16[32,8,32,128]{3,2,1,0:T(8,128)(2,1)S(1)}, u32[]{:S(2)}, u32[]{:S(2)}) %all-to-all-start.1) | async-done | bytes 2097184 | tf_op jit(solution)/shard_map/all_to_all | solution.py:133
  587.4 8.0 %select_reduce_fusion = bf16[32,8,32]{2,1,0:T(8,128)(2,1)S(1)} fusion(bf16[32,8,32,128]{3,2,1,0:T(8,128)(2,1)S(1)} %all-to-all-done.1, bf16[32,8,128,128]{3,2,1,0:T(8,128)(2,1)} %bitcast.87, pred[32,8,128]{2,1,0:T(8,128)(4,1)S(1)} %iota_compare_fusion.1), kind=kOutput, calls=%fused_computation.8 | convolution fusion | flops 270524416 | bytes 10534912 | tf_op jit(solution)/shard_map/snie,snte->snit/dot_general | solution.py:131
  596.0 7.8 %all-to-all-start.2 = ((bf16[32,2,128]{2,1,0:T(2,128)(2,1)}), bf16[32,2,128]{2,1,0:T(2,128)(2,1)S(1)}, u32[]{:S(2)}, u32[]{:S(2)}) async-start(bf16[32,2,128]{2,1,0:T(2,128)(2,1)} %reshape.374), calls=%async_computation.4 | async-start | bytes 32768 | tf_op jit(solution)/shard_map/all_to_all | solution.py:21
  603.8 8.6 %all-to-all-done.2 = bf16[32,2,128]{2,1,0:T(2,128)(2,1)S(1)} async-done(((bf16[32,2,128]{2,1,0:T(2,128)(2,1)}), bf16[32,2,128]{2,1,0:T(2,128)(2,1)S(1)}, u32[]{:S(2)}, u32[]{:S(2)}) %all-to-all-start.2) | async-done | bytes 16416 | tf_op jit(solution)/shard_map/all_to_all | solution.py:21
  (84 shorter events, 13.7 us)
Async XLA Ops:
  7.2 430.2 %copy-start = (s32[8192]{0:T(1024)S(1)}, s32[8192]{0:T(1024)}, u32[]{:S(2)}) copy-start(s32[8192]{0:T(1024)} %param.26) | copy-start | bytes 98308
  7.2 153.8 %all-gather.7.cloned.1.call-start = ((), (), s32[]{:S(2)}) async-start(), calls=%async_computation.5 | async-start | bytes 1179648 | tf_op jit(solution)/shard_map/all_gather | solution.py:45
  7.9 157.4 %all-gather.9.cloned.1.call-start = ((), (), s32[]{:S(2)}) async-start(), calls=%async_computation.6 | async-start | bytes 1081344 | tf_op jit(solution)/shard_map/all_gather | solution.py:48
  8.7 240.6 %reduce-scatter.3.cloned.1.call-start = ((), (), s32[]{:S(2)}) async-start(), calls=%async_computation.7 | async-start | bytes 1179648 | tf_op jit(solution)/shard_map/reduce_scatter | solution.py:85
  161.0 3.7 copy-start.3
  165.2 2.4 copy-start.7
  167.5 1.7 copy-start.4
  172.6 76.6 %copy-start.5 = (bf16[2,32,1024]{2,1,0:T(8,128)(2,1)S(1)}, bf16[2,32,1024]{2,1,0:T(8,128)(2,1)}, u32[]{:S(2)}) copy-start(bf16[2,32,1024]{2,1,0:T(8,128)(2,1)} %param.14) | copy-start | bytes 393220
  174.5 149.6 %all-gather.13.cloned.1.call-start = ((), (), s32[]{:S(2)}) async-start(), calls=%async_computation.9 | async-start | bytes 1081344 | tf_op jit(solution)/shard_map/all_gather | solution.py:91
  175.1 225.4 %all-gather.15.cloned.1.call-start = ((), (), s32[]{:S(2)}) async-start(), calls=%async_computation.10 | async-start | bytes 1081344 | tf_op jit(solution)/shard_map/all_gather | solution.py:94
  175.7 255.2 %all-gather.11.cloned.1.call-start = ((), (), s32[]{:S(2)}) async-start(), calls=%async_computation.8 | async-start | bytes 1179648 | tf_op jit(solution)/shard_map/all_gather | solution.py:90
  253.1 184.0 %copy-start.8 = (s32[2,16,4]{1,2,0:T(4,128)S(1)}, s32[2,16,4]{1,2,0:T(4,128)}, u32[]{:S(2)}) copy-start(s32[2,16,4]{1,2,0:T(4,128)} %param.27) | copy-start | bytes 1540
  253.1 197.2 %copy-start.9 = (bf16[4,128]{1,0:T(4,128)(2,1)S(1)}, bf16[4,128]{1,0:T(4,128)(2,1)}, u32[]{:S(2)}) copy-start(bf16[4,128]{1,0:T(4,128)(2,1)} %param.23) | copy-start | bytes 3076
  253.1 259.7 %reduce-scatter.5.cloned.1.call-start = ((), (), s32[]{:S(2)}) async-start(), calls=%async_computation.11 | async-start | bytes 1179648 | tf_op jit(solution)/shard_map/reduce_scatter | solution.py:96
  437.1 75.7 %copy-start.6 = (bf16[64,1024]{1,0:T(8,128)(2,1)S(1)}, bf16[64,1024]{1,0:T(8,128)(2,1)}, u32[]{:S(2)}) copy-start(bf16[64,1024]{1,0:T(8,128)(2,1)} %divide_convert_fusion.3) | copy-start | bytes 393220
  440.7 91.9 %all-to-all-start = ((s32[32,1,8]{2,1,0:T(1,128)}), s32[32,1,8]{2,1,0:T(1,128)S(1)}, u32[]{:S(2)}, u32[]{:S(2)}) async-start(s32[32,1,8]{2,1,0:T(1,128)} %bitcast.21), calls=%async_computation.2 | async-start | bytes 32768 | tf_op jit(solution)/shard_map/all_to_all | solution.py:128
  516.4 2.5 copy-start.2
  532.5 54.9 %all-to-all-start.1 = ((bf16[32,8,32,128]{3,2,1,0:T(8,128)(2,1)}), bf16[32,8,32,128]{3,2,1,0:T(8,128)(2,1)S(1)}, u32[]{:S(2)}, u32[]{:S(2)}) async-start(bf16[32,8,32,128]{3,2,1,0:T(8,128)(2,1)} %bitcast.24), calls=%async_computation.3 | async-start | bytes 4194304 | tf_op jit(solution)/shard_map/all_to_all | solution.py:133
  538.9 11.8 %copy-start.1 = (s32[256]{0:T(256)S(1)}, s32[256]{0:T(256)}, u32[]{:S(2)}) copy-start(s32[256]{0:T(256)} %param.25) | copy-start | bytes 3076
  596.0 16.4 %all-to-all-start.2 = ((bf16[32,2,128]{2,1,0:T(2,128)(2,1)}), bf16[32,2,128]{2,1,0:T(2,128)(2,1)S(1)}, u32[]{:S(2)}, u32[]{:S(2)}) async-start(bf16[32,2,128]{2,1,0:T(2,128)(2,1)} %reshape.374), calls=%async_computation.4 | async-start | bytes 32768 | tf_op jit(solution)/shard_map/all_to_all | solution.py:21
Sparse Core Ops, SparseCore 0:
  9.8 29.9 all-gather.6
  42.4 71.3 all-gather.8
  174.6 74.5 reduce-scatter.2
  251.7 72.3 all-gather.12
  326.6 73.8 all-gather.14
  402.1 28.6 all-gather.10
  437.2 32.1 reduce-scatter.4
where the time goes:
time: 622 us; the launch traced here: 621 us
  waiting for transfers between devices  297 us (48%)
  blocking collectives  215 us (35%)
  local copies, waits for them, and re-layouts  35.7 us (6%)
  matrix products  27.4 us (4%)
  starting transfers between devices  24 us (4%)
  between operations  14.6 us (2%)
  other arithmetic  7.57 us (1%)
    all_gather x1, waiting for transfers between devices, body(): lax.all_gather(w_down, 'dp', axis=1, tiled=True)  76.3 us
    reduce_scatter x1, waiting for transfers between devices, body(): lax.psum_scatter(attn_terms.astype(jnp.bfloat16), 'mp', scatter_dimension...  73.5 us
    all_gather x1, waiting for transfers between devices, body(): up = add_rows(mid_all, lax.all_gather(w_up, 'dp', axis=0, tiled=True))  70.8 us
    all_gather x1, blocking collectives, body(): lax.all_gather(w_proj, ('dp', 'mp'), axis=0, tiled=True)  62.5 us
    all_gather x1, blocking collectives, body(): lax.all_gather(query_weight, 'dp', axis=0, tiled=True)  41.4 us
    all_gather x1, blocking collectives, body(): lax.all_gather(w_key, 'dp', axis=0, tiled=True)  38.1 us
    all_gather x1, blocking collectives, body(): lax.all_gather(w_value, 'dp', axis=0, tiled=True)  37.2 us
    all_gather x1, blocking collectives, body(): lax.all_gather(w_out, 'dp', axis=1, tiled=True)  35.7 us
  transfers between devices with their start and end apart: 10, of which 6 were waited for; matrix products, arithmetic and copies ran while one was open for 7% of the time, Pallas kernels for 0%

commit v1 on v0

--- a/solution.py
+++ b/solution.py
@@ -4,6 +4,27 @@
 from jax.sharding import PartitionSpec as P
 
 HD = 64
+
+
+def ring_gather(value, axis, dim):
+    size, mine, rows = (lax.axis_size(axis), lax.axis_index(axis), value.shape[dim])
+    right = [(i, (i + 1) % size) for i in range(size)]
+    left = [(i, (i - 1) % size) for i in range(size)]
+    filled = jnp.zeros((*value.shape[:dim], size * rows, *value.shape[dim + 1 :]), value.dtype)
+    filled = lax.dynamic_update_slice_in_dim(filled, value, mine * rows, axis=dim)
+    from_left = from_right = value
+    halfway = size // 2
+    for step in range(1, halfway + 1):
+        from_left = lax.ppermute(from_left, axis, right)
+        filled = lax.dynamic_update_slice_in_dim(
+            filled, from_left, (mine - step) % size * rows, axis=dim
+        )
+        if step < size - halfway:
+            from_right = lax.ppermute(from_right, axis, left)
+            filled = lax.dynamic_update_slice_in_dim(
+                filled, from_right, (mine + step) % size * rows, axis=dim
+            )
+    return filled
 
 
 def layer_norm(value):
@@ -87,7 +108,7 @@
     ).astype(jnp.float32)
     own = hidden.reshape(qry_dev * qlen, width).astype(jnp.float32)
     mid = layer_norm(own + attn).astype(jnp.bfloat16)
-    mid_all = lax.all_gather(mid, "mp", axis=0, tiled=True)
+    mid_all = ring_gather(mid, "mp", 0)
     up = add_rows(mid_all, lax.all_gather(w_up, "dp", axis=0, tiled=True))
     inner = jax.nn.gelu(up, approximate=False).astype(jnp.bfloat16)
     down_terms = jnp.dot(

time: 622 us -> 595 us (0.957)
  waiting for transfers between devices: 297 us -> 254 us
  starting transfers between devices: 24 us -> 33.7 us
    all_gather x1 -> x0, waiting for transfers between devices: 30.5 us -> none  [body(): mid_all = lax.all_gather(mid, 'mp', axis=0, tiled=True)]
    all_gather x1, waiting for transfers between devices: 70.8 us -> 50.9 us  [body(): up = add_rows(mid_all, lax.all_gather(w_up, 'dp', axis=0, tiled=True))]
    ppermute x0 -> x7, starting transfers between devices: none -> 12.5 us  [the longest x3 9.5 us: ring_gather(): from_right = lax.ppermute(from_right, axis, left)]
    ppermute x0 -> x7, waiting for transfers between devices: none -> 7.98 us  [the longest x4 7.84 us: ring_gather(): from_left = lax.ppermute(from_left, axis, right)]
  transfers between devices with their start and end apart: 10 -> 16, of which waited for: 6 -> 10; matrix products, arithmetic and copies ran while one was open for 7% -> 8% of each run, Pallas kernels for 0% -> 0%
where the time goes in v1:
time: 595 us; the launch traced here: 594 us
  waiting for transfers between devices  254 us (43%)
  blocking collectives  221 us (37%)
  local copies, waits for them, and re-layouts  36.6 us (6%)
  starting transfers between devices  33.7 us (6%)
  matrix products  27.1 us (5%)
  between operations  14.6 us (2%)
  other arithmetic  6.92 us (1%)
    all_gather x1, waiting for transfers between devices, body(): lax.all_gather(w_down, 'dp', axis=1, tiled=True)  76.3 us
    reduce_scatter x1, waiting for transfers between devices, body(): lax.psum_scatter(attn_terms.astype(jnp.bfloat16), 'mp', scatter_dimension...  73.3 us
    all_gather x1, blocking collectives, body(): lax.all_gather(w_proj, ('dp', 'mp'), axis=0, tiled=True)  68.6 us
    all_gather x1, waiting for transfers between devices, body(): up = add_rows(mid_all, lax.all_gather(w_up, 'dp', axis=0, tiled=True))  50.9 us
    all_gather x1, blocking collectives, body(): lax.all_gather(query_weight, 'dp', axis=0, tiled=True)  41.4 us
    all_gather x1, blocking collectives, body(): lax.all_gather(w_key, 'dp', axis=0, tiled=True)  38.1 us
    all_gather x1, blocking collectives, body(): lax.all_gather(w_value, 'dp', axis=0, tiled=True)  37.2 us
    all_gather x1, blocking collectives, body(): lax.all_gather(w_out, 'dp', axis=1, tiled=True)  35.6 us
  transfers between devices with their start and end apart: 16, of which 10 were waited for; matrix products, arithmetic and copies ran while one was open for 8% of the time, Pallas kernels for 0%

profile of v1, /device:TPU:1, one launch (start us, length us, event | category | flops | bytes accessed | tf_op | source)
XLA Modules:
  0.0 593.9 jit_solution(11726428633923320065)
XLA Ops:
  8.7 41.4 %all_gather.29 = bf16[1024,128]{1,0:T(8,128)(2,1)S(1)} all-gather(bf16[32,128]{1,0:T(8,128)(2,1)} %param.15), channel_id=1, replica_groups=mesh['dp'=32,'mp'=8] {'dp'}, dimensions={0}, use_global_device_ids=true | all-gather | bytes 270336 | tf_op jit(solution)/shard_map/all_gather | solution.py:71
  50.1 38.1 %all_gather.30 = bf16[1024,128]{1,0:T(8,128)(2,1)S(1)} all-gather(bf16[32,128]{1,0:T(8,128)(2,1)} %param.16), channel_id=1, replica_groups=mesh['dp'=32,'mp'=8] {'dp'}, dimensions={0}, use_global_device_ids=true | all-gather | bytes 270336 | tf_op jit(solution)/shard_map/all_gather | solution.py:72
  88.1 37.2 %all_gather.28 = bf16[1024,128]{1,0:T(8,128)(2,1)S(1)} all-gather(bf16[32,128]{1,0:T(8,128)(2,1)} %param.17), channel_id=1, replica_groups=mesh['dp'=32,'mp'=8] {'dp'}, dimensions={0}, use_global_device_ids=true | all-gather | bytes 270336 | tf_op jit(solution)/shard_map/all_gather | solution.py:73
  125.3 35.6 %all_gather.32 = bf16[128,1024]{0,1:T(8,128)(2,1)S(1)} all-gather(bf16[128,32]{0,1:T(8,128)(2,1)} %param.20), channel_id=1, replica_groups=mesh['dp'=32,'mp'=8] {'dp'}, dimensions={1}, use_global_device_ids=true | all-gather | bytes 270336 | tf_op jit(solution)/shard_map/all_gather | solution.py:103
  160.9 1.7 convolution_convert_fusion.6
  162.8 1.7 convolution_convert_fusion.5
  166.0 1.7 convolution_convert_fusion.4
  168.2 1.4 fusion.3
  170.9 1.4 fusion.1
  173.7 1.4 convolution_convert_fusion
  176.5 73.3 %reduce-scatter.3.cloned.1.call-done = bf16[64,1024]{1,0:T(8,128)(2,1)} async-done(((bf16[512,1024]{1,0:T(8,128)(2,1)}), bf16[64,1024]{1,0:T(8,128)(2,1)}) %reduce-scatter.3.cloned.1.call-update) | async-done | bytes 131088 | tf_op jit(solution)/shard_map/reduce_scatter | solution.py:106
  254.2 2.0 collective-permute-start.1
  256.9 1.6 collective-permute-start.2
  258.6 3.2 collective-permute-start.3
  262.9 4.4 collective-permute-start.5
  268.3 5.4 collective-permute-done.6
  273.8 50.9 %all-gather.10.cloned.1.call-done = bf16[1024,512]{1,0:T(8,128)(2,1)} async-done(((bf16[32,512]{1,0:T(8,128)(2,1)}), bf16[1024,512]{1,0:T(8,128)(2,1)}) %all-gather.10.cloned.1.call-update) | async-done | bytes 1048592 | tf_op jit(solution)/shard_map/all_gather | solution.py:112
  324.7 76.3 %all-gather.12.cloned.1.call-done = bf16[512,1024]{0,1:T(8,128)(2,1)} async-done(((bf16[512,32]{0,1:T(8,128)(2,1)}), bf16[512,1024]{0,1:T(8,128)(2,1)}) %all-gather.12.cloned.1.call-update) | async-done | bytes 1048592 | tf_op jit(solution)/shard_map/all_gather | solution.py:115
  401.1 5.9 convolution_convert_fusion.1
  407.2 1.1 gather_fusion
  410.5 6.0 %all-to-all-start = ((s32[32,1,8]{2,1,0:T(1,128)}), s32[32,1,8]{2,1,0:T(1,128)S(1)}, u32[]{:S(2)}, u32[]{:S(2)}) async-start(s32[32,1,8]{2,1,0:T(1,128)} %bitcast.21), calls=%async_computation.2 | async-start | bytes 32768 | tf_op jit(solution)/shard_map/all_to_all | solution.py:149
  416.6 68.6 %all-gather = bf16[256,4,128]{2,1,0:T(4,128)(2,1)S(1)} all-gather(bf16[1,4,128]{2,1,0:T(4,128)(2,1)S(1)} %bitcast.96), channel_id=1, replica_groups=mesh['dp'=32,'mp'=8] {'dp','mp'}, dimensions={0}, use_global_device_ids=true | all-gather | bytes 263168 | tf_op jit(solution)/shard_map/all_gather | solution.py:122
  487.4 1.3 multiply_reduce_fusion.2
  489.6 1.7 broadcast_in_dim.17
  491.2 13.7 %scatter_fusion = bf16[256,32,128]{2,1,0:T(8,128)(2,1)} fusion(bf16[256,32,128]{2,1,0:T(8,128)(2,1)} %broadcast_in_dim.17, s32[128]{0:T(128)S(1)} %fusion.75, bf16[128,32,128]{2,1,0:T(8,128)(2,1)S(1)} %gather_fusion.2), kind=kCustom, calls=%fused_computation.6 | custom fusion | bytes 3146240 | tf_op jit(solution)/shard_map/scatter | solution.py:146
  504.9 6.9 %all-to-all-start.1 = ((bf16[32,8,32,128]{3,2,1,0:T(8,128)(2,1)}), bf16[32,8,32,128]{3,2,1,0:T(8,128)(2,1)S(1)}, u32[]{:S(2)}, u32[]{:S(2)}) async-start(bf16[32,8,32,128]{3,2,1,0:T(8,128)(2,1)} %bitcast.24), calls=%async_computation.3 | async-start | bytes 4194304 | tf_op jit(solution)/shard_map/all_to_all | solution.py:154
  512.0 11.8 %gather_fusion.3 = bf16[256,128,128]{2,1,0:T(8,128)(2,1)} fusion(bf16[256,128,128]{2,1,0:T(8,128)(2,1)} %param.24, s32[1024]{0:T(1024)S(1)} %pad_clamp_fusion.2), kind=kCustom, calls=%fused_computation.3 | custom fusion | bytes 16778240 | tf_op jit(solution)/shard_map/gather | solution.py:150
  523.9 1.9 gather_fusion.1
  526.0 34.5 %all-to-all-done.1 = bf16[32,8,32,128]{3,2,1,0:T(8,128)(2,1)S(1)} async-done(((bf16[32,8,32,128]{3,2,1,0:T(8,128)(2,1)}), bf16[32,8,32,128]{3,2,1,0:T(8,128)(2,1)S(1)}, u32[]{:S(2)}, u32[]{:S(2)}) %all-to-all-start.1) | async-done | bytes 2097184 | tf_op jit(solution)/shard_map/all_to_all | solution.py:154
  560.5 8.0 %select_reduce_fusion = bf16[32,8,32]{2,1,0:T(8,128)(2,1)S(1)} fusion(bf16[32,8,32,128]{3,2,1,0:T(8,128)(2,1)S(1)} %all-to-all-done.1, bf16[32,8,128,128]{3,2,1,0:T(8,128)(2,1)} %bitcast.87, pred[32,8,128]{2,1,0:T(8,128)(4,1)S(1)} %iota_compare_fusion.1), kind=kOutput, calls=%fused_computation.8 | convolution fusion | flops 270524416 | bytes 10534912 | tf_op jit(solution)/shard_map/snie,snte->snit/dot_general | solution.py:152
  569.1 7.8 %all-to-all-start.2 = ((bf16[32,2,128]{2,1,0:T(2,128)(2,1)}), bf16[32,2,128]{2,1,0:T(2,128)(2,1)S(1)}, u32[]{:S(2)}, u32[]{:S(2)}) async-start(bf16[32,2,128]{2,1,0:T(2,128)(2,1)} %reshape.374), calls=%async_computation.4 | async-start | bytes 32768 | tf_op jit(solution)/shard_map/all_to_all | solution.py:42
  576.9 8.6 %all-to-all-done.2 = bf16[32,2,128]{2,1,0:T(2,128)(2,1)S(1)} async-done(((bf16[32,2,128]{2,1,0:T(2,128)(2,1)}), bf16[32,2,128]{2,1,0:T(2,128)(2,1)S(1)}, u32[]{:S(2)}, u32[]{:S(2)}) %all-to-all-start.2) | async-done | bytes 16416 | tf_op jit(solution)/shard_map/all_to_all | solution.py:42
  (102 shorter events, 22.7 us)
Async XLA Ops:
  7.2 400.1 %copy-start = (s32[8192]{0:T(1024)S(1)}, s32[8192]{0:T(1024)}, u32[]{:S(2)}) copy-start(s32[8192]{0:T(1024)} %param.26) | copy-start | bytes 98308
  7.2 153.8 %all-gather.6.cloned.1.call-start = ((), (), s32[]{:S(2)}) async-start(), calls=%async_computation.5 | async-start | bytes 1179648 | tf_op jit(solution)/shard_map/all_gather | solution.py:66
  7.9 158.1 %all-gather.8.cloned.1.call-start = ((), (), s32[]{:S(2)}) async-start(), calls=%async_computation.6 | async-start | bytes 1081344 | tf_op jit(solution)/shard_map/all_gather | solution.py:69
  8.7 241.2 %reduce-scatter.3.cloned.1.call-start = ((), (), s32[]{:S(2)}) async-start(), calls=%async_computation.7 | async-start | bytes 1179648 | tf_op jit(solution)/shard_map/reduce_scatter | solution.py:106
  160.9 3.7 copy-start.3
  165.1 3.1 copy-start.7
  168.2 1.7 copy-start.4
  170.9 2.1 copy-start.6
  173.3 76.6 %copy-start.5 = (bf16[2,32,1024]{2,1,0:T(8,128)(2,1)S(1)}, bf16[2,32,1024]{2,1,0:T(8,128)(2,1)}, u32[]{:S(2)}) copy-start(bf16[2,32,1024]{2,1,0:T(8,128)(2,1)} %param.14) | copy-start | bytes 393220
  175.1 149.6 %all-gather.10.cloned.1.call-start = ((), (), s32[]{:S(2)}) async-start(), calls=%async_computation.8 | async-start | bytes 1081344 | tf_op jit(solution)/shard_map/all_gather | solution.py:112
  175.7 225.3 %all-gather.12.cloned.1.call-start = ((), (), s32[]{:S(2)}) async-start(), calls=%async_computation.9 | async-start | bytes 1081344 | tf_op jit(solution)/shard_map/all_gather | solution.py:115
  176.3 308.9 %reduce-scatter.5.cloned.1.call-start = ((), (), s32[]{:S(2)}) async-start(), calls=%async_computation.10 | async-start | bytes 1179648 | tf_op jit(solution)/shard_map/reduce_scatter | solution.py:117
  253.2 3.8 collective-permute-start
  254.2 4.4 collective-permute-start.1
  256.9 5.6 collective-permute-start.2
  258.6 4.4 collective-permute-start.3
  262.5 5.6 collective-permute-start.4
  262.9 5.4 collective-permute-start.5
  268.2 5.6 collective-permute-start.6
  273.8 133.2 %copy-start.8 = (s32[2,16,4]{1,2,0:T(4,128)S(1)}, s32[2,16,4]{1,2,0:T(4,128)}, u32[]{:S(2)}) copy-start(s32[2,16,4]{1,2,0:T(4,128)} %param.27) | copy-start | bytes 1540
  273.8 142.8 %copy-start.9 = (bf16[4,128]{1,0:T(4,128)(2,1)S(1)}, bf16[4,128]{1,0:T(4,128)(2,1)}, u32[]{:S(2)}) copy-start(bf16[4,128]{1,0:T(4,128)(2,1)} %param.23) | copy-start | bytes 3076
  410.5 94.4 %all-to-all-start = ((s32[32,1,8]{2,1,0:T(1,128)}), s32[32,1,8]{2,1,0:T(1,128)S(1)}, u32[]{:S(2)}, u32[]{:S(2)}) async-start(s32[32,1,8]{2,1,0:T(1,128)} %bitcast.21), calls=%async_computation.2 | async-start | bytes 32768 | tf_op jit(solution)/shard_map/all_to_all | solution.py:149
  488.8 2.5 copy-start.2
  504.9 55.5 %all-to-all-start.1 = ((bf16[32,8,32,128]{3,2,1,0:T(8,128)(2,1)}), bf16[32,8,32,128]{3,2,1,0:T(8,128)(2,1)S(1)}, u32[]{:S(2)}, u32[]{:S(2)}) async-start(bf16[32,8,32,128]{3,2,1,0:T(8,128)(2,1)} %bitcast.24), calls=%async_computation.3 | async-start | bytes 4194304 | tf_op jit(solution)/shard_map/all_to_all | solution.py:154
  512.0 11.8 %copy-start.1 = (s32[256]{0:T(256)S(1)}, s32[256]{0:T(256)}, u32[]{:S(2)}) copy-start(s32[256]{0:T(256)} %param.25) | copy-start | bytes 3076
  569.1 16.4 %all-to-all-start.2 = ((bf16[32,2,128]{2,1,0:T(2,128)(2,1)}), bf16[32,2,128]{2,1,0:T(2,128)(2,1)S(1)}, u32[]{:S(2)}, u32[]{:S(2)}) async-start(bf16[32,2,128]{2,1,0:T(2,128)(2,1)} %reshape.374), calls=%async_computation.4 | async-start | bytes 32768 | tf_op jit(solution)/shard_map/all_to_all | solution.py:42
Sparse Core Ops, SparseCore 0:
  9.8 29.9 all-gather.5
  42.4 71.4 all-gather.7
  175.3 74.5 reduce-scatter.2
  252.3 72.4 all-gather.9
  327.2 73.8 all-gather.11
  407.1 35.2 reduce-scatter.4
